TPU v7x, 256 devices: a whole 4x4x8 slice. The times are simulated.
256 devices in a mesh: dp: 16 (over z, core), help: 16 (over y, x).
Axes of the slice: x: 4, y: 4, z: 8, core: 2. Of those that a mesh axis runs over, the one named last changes fastest.
Arguments:
- queries: bfloat16 [65536, 16, 128], P(('dp', 'help')), may hold values from -48 to 48
- keys_values: bfloat16 [65536, 4, 256], P(('dp', 'help')), may hold values from -4 to 4
- segment_ids: int32 [16, 4096], P('dp', 'help'), may hold values from 0 to 3, never falling along the last dimension, each value on 1 to 2048 neighbouring positions
- residual: bfloat16 [65536, 4096], P(('dp', 'help')), may hold values from -3 to 3
- out_weight: bfloat16 [2048, 4096], P(None, 'dp'), may hold values from -1 to 1
Outputs:
- layer_out: bfloat16 [65536, 4096], P(('dp', 'help'))
All inputs are finite; a program needn't handle non-finite values.
Results may differ from a plain program's by a relative error of at most 0.0085.
Values may be sent and summed in bfloat16 or wider, within the bound.
No kernel may reach another device: no remote copies, remote signals or barrier semaphores. Data moves between devices by JAX's collectives and lax.ppermute only.
A program may use at most 128 MiB of HBM per device.

v0:
```python
import functools
import math

import jax
import jax.numpy as jnp
from jax import lax
from jax.experimental import pallas as pl
from jax.experimental.pallas import tpu as pltpu
from jax.sharding import Mesh
from jax.sharding import PartitionSpec as P

masked_score = -1e30
MOST = 2048
SEG_ROWS = 16
INTERPRET = False
QUERY_CHUNK = 128


def attention_kernel(
    flags_ref, q_ref, segq_ref, segk_ref, *refs, blocks, group_size, head_dim, score_scale
):
    kv_refs = refs[:blocks]
    o_ref = refs[blocks]
    m_ref, acc_ref = refs[blocks + 1 :]
    rows = q_ref.shape[0]
    chunks = rows // QUERY_CHUNK
    lanes = m_ref.shape[1]
    exp2_scale = score_scale * math.log2(math.e)
    m_ref[...] = jnp.full(m_ref.shape, masked_score, jnp.float32)
    acc_ref[...] = jnp.zeros(acc_ref.shape, jnp.float32)
    ones = jnp.ones((rows, head_dim), jnp.bfloat16)

    for s in range(blocks):

        def step(s=s):
            keys = kv_refs[s][:, :head_dim]
            values = jnp.concatenate([kv_refs[s][:, head_dim:], ones], axis=1)
            segk = segk_ref[s : s + 1, :]
            for c in range(chunks):
                lo = c * QUERY_CHUNK
                allowed = segq_ref[lo : lo + QUERY_CHUNK, :] == segk
                if s == 0:
                    qi = lax.broadcasted_iota(jnp.int32, (QUERY_CHUNK, rows), 0) + lo
                    ki = lax.broadcasted_iota(jnp.int32, (QUERY_CHUNK, rows), 1)
                    allowed = jnp.logical_and(allowed, ki <= qi)
                bias = jnp.where(allowed, 0.0, masked_score).astype(jnp.float32)
                for h in range(group_size):
                    part = q_ref[lo : lo + QUERY_CHUNK, h * head_dim : (h + 1) * head_dim]
                    scores = (
                        lax.dot_general(
                            part,
                            keys,
                            (((1,), (1,)), ((), ())),
                            preferred_element_type=jnp.float32,
                        )
                        + bias
                    )
                    r = slice(h * rows + lo, h * rows + lo + QUERY_CHUNK)
                    m_old = m_ref[r, :]
                    m_new = jnp.maximum(m_old, jnp.max(scores, axis=1, keepdims=True))
                    wide = jnp.concatenate([m_new] * (rows // lanes), axis=1)
                    weights = jnp.exp2((scores - wide) * exp2_scale)
                    factor = jnp.exp2((m_old - m_new) * exp2_scale)
                    factor = jnp.concatenate([factor] * (2 * head_dim // lanes), axis=1)
                    acc_ref[r, :] = acc_ref[r, :] * factor + jnp.dot(
                        weights.astype(jnp.bfloat16), values, preferred_element_type=jnp.float32
                    )
                    m_ref[r, :] = m_new

        if s == 0:
            step()
        else:
            pl.when(flags_ref[s] > 0)(step)

    for h in range(group_size):
        r = slice(h * rows, (h + 1) * rows)
        acc = acc_ref[r, :]
        o_ref[:, h * head_dim : (h + 1) * head_dim] = (
            acc[:, :head_dim] / acc[:, head_dim:]
        ).astype(o_ref.dtype)


def tokens_attention(queries, keys_values, seg_local, helper, help_size):
    local_rows, heads, head_dim = queries.shape
    heads_kv = keys_values.shape[1]
    group_size = heads // heads_kv
    pair = keys_values.shape[2]
    score_scale = 1.0 / math.sqrt(head_dim)
    flat = keys_values.reshape(local_rows, heads_kv * pair)
    seg_row = jnp.zeros((SEG_ROWS, heads_kv * pair), jnp.bfloat16)
    seg_row = seg_row.at[0, :local_rows].set(seg_local.astype(jnp.bfloat16))
    packed = jnp.concatenate([flat, seg_row], axis=0)
    reach = min((MOST - 1 + local_rows - 1) // local_rows, help_size - 1)
    across = math.isqrt(help_size)
    one_back = lax.ppermute(
        packed, "help", [(j, j + across) for j in range(help_size - across)]
    )
    two_back = lax.ppermute(
        packed, "help", [(j, j + 2 * across) for j in range(help_size - 2 * across)]
    )
    column = helper % across
    pieces = {0: packed, across: one_back, 2 * across: two_back}
    for k in range(1, across):
        pairs = [
            (y * across + x, y * across + (x + k) % across)
            for y in range(help_size // across)
            for x in range(across)
        ]
        wraps = column + k >= across
        sent = jnp.where(
            wraps, jnp.stack([one_back, two_back]), jnp.stack([packed, one_back])
        )
        got = lax.ppermute(sent, "help", pairs)
        pieces[k] = got[0]
        pieces[k + across] = got[1]
    received = [pieces[s] for s in range(reach + 1)]
    blocks = len(received)
    segk = jnp.stack(
        [seg_local] + [r[local_rows, :local_rows].astype(jnp.int32) for r in received[1:]]
    )
    first_seg = seg_local[0]
    flags = jnp.stack(
        [jnp.int32(1)]
        + [
            jnp.logical_and(helper >= s, segk[s, local_rows - 1] >= first_seg).astype(jnp.int32)
            for s in range(1, blocks)
        ]
    )
    kernel = functools.partial(
        attention_kernel,
        blocks=blocks,
        group_size=group_size,
        head_dim=head_dim,
        score_scale=score_scale,
    )
    width = group_size * head_dim
    grid_spec = pltpu.PrefetchScalarGridSpec(
        num_scalar_prefetch=1,
        grid=(heads_kv,),
        in_specs=[
            pl.BlockSpec((local_rows, width), lambda g, f: (0, g)),
            pl.BlockSpec((local_rows, 1), lambda g, f: (0, 0)),
            pl.BlockSpec((blocks, local_rows), lambda g, f: (0, 0)),
        ]
        + [pl.BlockSpec((local_rows, pair), lambda g, f: (0, g)) for _ in range(blocks)],
        out_specs=pl.BlockSpec((local_rows, width), lambda g, f: (0, g)),
        scratch_shapes=[
            pltpu.VMEM((group_size * local_rows, 128), jnp.float32),
            pltpu.VMEM((group_size * local_rows, 2 * head_dim), jnp.float32),
        ],
    )
    return pl.pallas_call(
        kernel,
        grid_spec=grid_spec,
        out_shape=jax.ShapeDtypeStruct((local_rows, heads * head_dim), jnp.bfloat16),
        compiler_params=pltpu.CompilerParams(dimension_semantics=("arbitrary",)),
        interpret=INTERPRET,
    )(
        flags,
        queries.reshape(local_rows, heads * head_dim),
        seg_local.reshape(local_rows, 1),
        segk,
        *received,
    )


def make_on_device(help_size):
    partner = [(0, 1), (1, 0)]

    def on_device(queries, keys_values, segment_ids, residual, out_weight):
        local_rows = queries.shape[0]
        width = out_weight.shape[1]
        gathered = lax.all_gather(out_weight, "z", axis=0)
        seg_local = segment_ids.reshape(local_rows)
        helper = lax.axis_index("help")
        core = lax.axis_index("core")
        first = core == 0
        planes = gathered.shape[0]
        stream = residual.reshape(local_rows, planes, 2, width)
        own_cols = jnp.where(first, stream[:, :, 0], stream[:, :, 1])
        other_cols = jnp.where(first, stream[:, :, 1], stream[:, :, 0])
        partner_res = lax.ppermute(other_cols, "core", partner)
        attended = tokens_attention(queries, keys_values, seg_local, helper, help_size)
        partner_att = lax.ppermute(attended, "core", partner)

        def project(rows, res):
            summed = jnp.einsum(
                "qk,zkn->qzn", rows, gathered, preferred_element_type=jnp.float32
            )
            return (res.astype(jnp.float32) + summed).astype(jnp.bfloat16)

        mine = project(attended, own_cols)
        theirs = project(partner_att, partner_res)
        back = lax.ppermute(theirs, "core", partner)
        col0 = jnp.where(first, mine, back)
        col1 = jnp.where(first, back, mine)
        return jnp.stack([col0, col1], axis=2).reshape(local_rows, planes * 2 * width)

    return on_device


def solution(mesh):
    dp_size, help_size = mesh.devices.shape
    split = Mesh(mesh.devices.reshape(dp_size // 2, 2, help_size), ("z", "core", "help"))
    rows = ("z", "core", "help")
    return jax.shard_map(
        make_on_device(help_size),
        mesh=split,
        in_specs=(
            P(rows, None, None),
            P(rows, None, None),
            P(("z", "core"), "help"),
            P(rows, None),
            P(None, ("z", "core")),
        ),
        out_specs=P(rows, None),
        check_vma=False,
    )
```

profile of v0, /device:TPU:241, one launch (start us, length us, event | category | flops | bytes accessed | tf_op | source)
XLA Modules:
  0.0 166.3 jit_solution(13520813344944159975)
XLA Ops:
  6.5 0.0 all-gather.3.cloned.1.call-start
  6.5 0.7 all-gather.3.cloned.1.call-update
  7.3 1.1 copy.20
  8.4 0.1 fusion.8
  8.6 2.9 %collective-permute-start = (bf16[272,1024]{1,0:T(8,128)(2,1)S(1)}, bf16[272,1024]{1,0:T(8,128)(2,1)S(1)}, u32[]{:S(2)}, u32[]{:S(2)}) collective-permute-start(bf16[272,1024]{1,0:T(8,128)(2,1)S(1)} %get-tuple-element.29.refs_0_), channel_id=1, source_target_pairs={{0,4},{1,5},{2,6},{3,7},{4,8},{5,9},{6,10},{7,11},{8,12},{9,13},{1... | collective-permute-start | bytes 1671176 | tf_op jit(solution)/shard_map/ppermute | solution.py:95
  11.5 1.3 collective-permute-start.1
  12.8 11.4 %collective-permute-done.refs_4_ = bf16[272,1024]{1,0:T(8,128)(2,1)S(1)} collective-permute-done((bf16[272,1024]{1,0:T(8,128)(2,1)S(1)}, bf16[272,1024]{1,0:T(8,128)(2,1)S(1)}, u32[]{:S(2)}, u32[]{:S(2)}) %collective-permute-start) | collective-permute-done | bytes 557088 | tf_op jit(solution)/shard_map/ppermute | solution.py:95
  24.2 11.8 %collective-permute-done.1.refs_8_ = bf16[272,1024]{1,0:T(8,128)(2,1)S(1)} collective-permute-done((bf16[272,1024]{1,0:T(8,128)(2,1)S(1)}, bf16[272,1024]{1,0:T(8,128)(2,1)S(1)}, u32[]{:S(2)}, u32[]{:S(2)}) %collective-permute-start.1) | collective-permute-done | bytes 557088 | tf_op jit(solution)/shard_map/ppermute | solution.py:98
  35.9 2.1 %broadcast_select_fusion = (bf16[2,272,1024]{2,1,0:T(8,128)(2,1)}, bf16[2,272,1024]{2,1,0:T(8,128)(2,1)}, bf16[2,272,1024]{2,1,0:T(8,128)(2,1)}) fusion(pred[]{:T(512)S(6)} %ge.90, bf16[1,272,1024]{2,1,0:T(8,128)(2,1)S(1)} %bitcast.85, bf16[1,272,1024]{2,1,0:T(8,128)(2,1)S(1)} %get-tuple-element.28, bf16[1,272,1024]{2,1,0:T(8,128)(2,1)S(1)} %bitcast.86, ...), kind=kLoop, calls=%fused_computation.8 | loop fusion | flops 2785280 | bytes 5013507 | tf_op jit(solution)/shard_map/jit(_where)/select_n | solution.py:110
  38.0 2.5 %collective-permute-start.4 = (bf16[2,272,1024]{2,1,0:T(8,128)(2,1)}, bf16[2,272,1024]{2,1,0:T(8,128)(2,1)}, u32[]{:S(2)}, u32[]{:S(2)}) collective-permute-start(bf16[2,272,1024]{2,1,0:T(8,128)(2,1)} %get-tuple-element.19), channel_id=1, source_target_pairs={{0,3},{1,0},{2,1},{3,2},{4,7},{5,4},{6,5},{7,6},{8,11},{9,8},{10,9... | collective-permute-start | bytes 3342344 | tf_op jit(solution)/shard_map/ppermute | solution.py:113
  40.5 3.3 %copy.8 = bf16[256,4096]{0,1:T(8,128)(2,1)S(1)} copy(bf16[256,4096]{1,0:T(8,128)(2,1)} %param.10) | data formatting | bytes 4194304 | tf_op args[3]
  43.8 0.6 collective-permute-start.3
  44.4 1.1 select_bitcast_fusion.2
  45.5 2.1 %collective-permute-start.5 = (bf16[256,8,256]{0,2,1:T(8,128)(2,1)}, bf16[256,8,256]{0,2,1:T(8,128)(2,1)}, u32[]{:S(2)}, u32[]{:S(2)}) collective-permute-start(bf16[256,8,256]{0,2,1:T(8,128)(2,1)} %select_bitcast_fusion.2), channel_id=1, source_target_pairs={{0,16},{16,0},{1,17},{17,1},{2,18},{18,2},{3,19},{19,3},{4,20},{20... | collective-permute-start | bytes 3145736 | tf_op jit(solution)/shard_map/ppermute | solution.py:182
  47.6 0.6 slice.99
  48.2 2.5 %copy.23 = bf16[32,8,16,128]{3,1,2,0:T(8,128)(2,1)} copy(bf16[32,8,16,128]{3,2,1,0:T(8,128)(2,1)} %bitcast.88) | data formatting | bytes 2097152
  50.7 0.8 copy.11.segq_ref
  51.5 0.6 collective-permute-start.2
  52.1 0.7 slice.131
  52.8 0.6 slice.142
  56.1 7.9 %collective-permute-done.4 = bf16[2,272,1024]{2,1,0:T(8,128)(2,1)} collective-permute-done((bf16[2,272,1024]{2,1,0:T(8,128)(2,1)}, bf16[2,272,1024]{2,1,0:T(8,128)(2,1)}, u32[]{:S(2)}, u32[]{:S(2)}) %collective-permute-start.4) | collective-permute-done | bytes 1114144 | tf_op jit(solution)/shard_map/ppermute | solution.py:113
  64.0 1.3 slice_bitcast_fusion.2
  65.3 0.8 slice.140
  66.1 0.7 slice.129
  66.7 3.3 %collective-permute-done.3 = bf16[2,272,1024]{2,1,0:T(8,128)(2,1)} collective-permute-done((bf16[2,272,1024]{2,1,0:T(8,128)(2,1)}, bf16[2,272,1024]{2,1,0:T(8,128)(2,1)}, u32[]{:S(2)}, u32[]{:S(2)}) %collective-permute-start.3) | collective-permute-done | bytes 1114144 | tf_op jit(solution)/shard_map/ppermute | solution.py:113
  70.1 1.3 slice_bitcast_fusion.3
  71.4 0.7 slice.137
  72.2 0.6 slice.126
  72.8 23.3 %collective-permute-done.2 = bf16[2,272,1024]{2,1,0:T(8,128)(2,1)} collective-permute-done((bf16[2,272,1024]{2,1,0:T(8,128)(2,1)}, bf16[2,272,1024]{2,1,0:T(8,128)(2,1)}, u32[]{:S(2)}, u32[]{:S(2)}) %collective-permute-start.2) | collective-permute-done | bytes 1114144 | tf_op jit(solution)/shard_map/ppermute | solution.py:113
  96.1 1.3 slice_bitcast_fusion.4
  97.5 0.7 copy-done.6
  98.3 0.3 copy-done.7
  98.5 0.6 slice.134
  99.2 1.2 stack.100.segk_ref
  100.4 0.6 slice.123
  109.0 0.1 stack.98
  109.1 0.6 stack.99.flags_ref
  109.7 7.2 %shard_map.55 = bf16[256,2048]{1,0:T(8,128)(2,1)} custom-call(s32[9]{0:T(128)} %stack.99.flags_ref, bf16[256,2048]{1,0:T(8,128)(2,1)} %bitcast.84, s32[256,1]{1,0:T(8,128)} %copy.11.segq_ref, s32[9,256]{1,0:T(8,128)} %stack.100.segk_ref, bf16[272,1024]{1,0:T(8,128)(2,1)} %copy-done.8, bf16[272,1024]{1,0:T(8,128)(2,1)} %copy-done.7, ...), custom_call_target="tpu_custom_call" | custom-call | tf_op jit(solution)/shard_map/pallas_call | solution.py:152
  116.9 23.2 %collective-permute-start.6 = (bf16[256,2048]{1,0:T(8,128)(2,1)}, bf16[256,2048]{1,0:T(8,128)(2,1)S(1)}, u32[]{:S(2)}, u32[]{:S(2)}) collective-permute-start(bf16[256,2048]{1,0:T(8,128)(2,1)} %shard_map.55), channel_id=1, source_target_pairs={{0,16},{16,0},{1,17},{17,1},{2,18},{18,2},{3,19},{19,3},{4,20},{20... | collective-permute-start | bytes 3145736 | tf_op jit(solution)/shard_map/ppermute | solution.py:184
  140.1 0.0 collective-permute-done.5
  140.1 2.5 %collective-permute-done.6 = bf16[256,2048]{1,0:T(8,128)(2,1)S(1)} collective-permute-done((bf16[256,2048]{1,0:T(8,128)(2,1)}, bf16[256,2048]{1,0:T(8,128)(2,1)S(1)}, u32[]{:S(2)}, u32[]{:S(2)}) %collective-permute-start.6) | collective-permute-done | bytes 1048608 | tf_op jit(solution)/shard_map/ppermute | solution.py:184
  142.6 7.2 %add_convert_fusion = bf16[256,8,256]{0,2,1:T(8,128)(2,1)S(1)} fusion(bf16[256,8,256]{0,2,1:T(8,128)(2,1)} %collective-permute-done.5, bf16[8,2048,256]{2,1,0:T(8,128)(2,1)} %bitcast.91, bf16[256,2048]{1,0:T(8,128)(2,1)S(1)} %collective-permute-done.6), kind=kOutput, calls=%fused_computation.3 | convolution fusion | flops 2149056512 | bytes 11534336 | tf_op jit(solution)/shard_map/qk,zkn->qzn/dot_general | solution.py:187
  149.7 0.5 collective-permute-start.7
  150.2 2.3 %collective-permute-done.7 = bf16[256,8,256]{0,2,1:T(8,128)(2,1)S(1)} collective-permute-done((bf16[256,8,256]{0,2,1:T(8,128)(2,1)S(1)}, bf16[256,8,256]{0,2,1:T(8,128)(2,1)S(1)}, u32[]{:S(2)}, u32[]{:S(2)}) %collective-permute-start.7) | collective-permute-done | bytes 1048608 | tf_op jit(solution)/shard_map/ppermute | solution.py:194
  152.5 3.7 %select_bitcast_fusion.1 = (bf16[256,8,1,256]{0,3,1,2:T(8,128)(2,1)S(1)}, bf16[256,8,1,256]{0,3,1,2:T(8,128)(2,1)S(1)}) fusion(bf16[256,8,256]{0,2,1:T(8,128)(2,1)S(1)} %collective-permute-done.7, pred[]{:T(512)S(6)} %eq.5, bf16[8,2048,256]{2,1,0:T(8,128)(2,1)S(1)} %bitcast.92, bf16[256,2048]{1,0:T(8,128)(2,1)S(1)} %copy-done.9, ...), kind=kOutput, calls=%fused_computation.18 | convolution fusion | flops 2150629376 | bytes 14681088 | tf_op jit(solution)/shard_map/qk,zkn->qzn/dot_general | solution.py:187
  156.2 0.2 pad_maximum_fusion
  156.4 0.1 copy.14
  156.6 2.9 %copy.15 = bf16[256,4096]{1,0:T(8,128)(2,1)} copy(bf16[256,4096]{0,1:T(8,128)(2,1)S(1)} %bitcast.83) | data formatting | bytes 4194304 | tf_op jit(solution)/shard_map/reshape | solution.py:197
  (29 shorter events, 0.1 us)
Async XLA Ops:
  6.5 1.9 %copy-start.10 = (s32[1,256]{1,0:T(1,128)S(1)}, s32[1,256]{1,0:T(1,128)}, u32[]{:S(2)}) copy-start(s32[1,256]{1,0:T(1,128)} %param.9) | copy-start | bytes 3076
  6.5 136.0 %all-gather.3.cloned.1.call-start = ((), (), s32[]{:S(2)}) async-start(), calls=%async_computation | async-start | bytes 9437184 | tf_op jit(solution)/shard_map/all_gather | solution.py:173
  8.6 29.5 %copy-start.8 = (bf16[272,1024]{1,0:T(8,128)(2,1)}, bf16[272,1024]{1,0:T(8,128)(2,1)S(1)}, u32[]{:S(2)}) copy-start(bf16[272,1024]{1,0:T(8,128)(2,1)S(1)} %get-tuple-element.29.refs_0_) | copy-start | bytes 1671172
  8.6 15.6 %collective-permute-start = (bf16[272,1024]{1,0:T(8,128)(2,1)S(1)}, bf16[272,1024]{1,0:T(8,128)(2,1)S(1)}, u32[]{:S(2)}, u32[]{:S(2)}) collective-permute-start(bf16[272,1024]{1,0:T(8,128)(2,1)S(1)} %get-tuple-element.29.refs_0_), channel_id=1, source_target_pairs={{0,4},{1,5},{2,6},{3,7},{4,8},{5,9},{6,10},{7,11},{8,12},{9,13},{1... | collective-permute-start | bytes 1671176 | tf_op jit(solution)/shard_map/ppermute | solution.py:95
  11.5 24.5 %collective-permute-start.1 = (bf16[272,1024]{1,0:T(8,128)(2,1)S(1)}, bf16[272,1024]{1,0:T(8,128)(2,1)S(1)}, u32[]{:S(2)}, u32[]{:S(2)}) collective-permute-start(bf16[272,1024]{1,0:T(8,128)(2,1)S(1)} %get-tuple-element.29.refs_0_), channel_id=1, source_target_pairs={{0,8},{1,9},{2,10},{3,11},{4,12},{5,13},{6,14},{7,15},{16,24},{17,... | collective-permute-start | bytes 1671176 | tf_op jit(solution)/shard_map/ppermute | solution.py:98
  24.2 27.9 %copy-start = (bf16[272,1024]{1,0:T(8,128)(2,1)}, bf16[272,1024]{1,0:T(8,128)(2,1)S(1)}, u32[]{:S(2)}) copy-start(bf16[272,1024]{1,0:T(8,128)(2,1)S(1)} %collective-permute-done.refs_4_) | copy-start | bytes 1671172
  35.9 16.8 %copy-start.1 = (bf16[272,1024]{1,0:T(8,128)(2,1)}, bf16[272,1024]{1,0:T(8,128)(2,1)S(1)}, u32[]{:S(2)}) copy-start(bf16[272,1024]{1,0:T(8,128)(2,1)S(1)} %collective-permute-done.1.refs_8_) | copy-start | bytes 1671172
  38.0 26.0 %collective-permute-start.4 = (bf16[2,272,1024]{2,1,0:T(8,128)(2,1)}, bf16[2,272,1024]{2,1,0:T(8,128)(2,1)}, u32[]{:S(2)}, u32[]{:S(2)}) collective-permute-start(bf16[2,272,1024]{2,1,0:T(8,128)(2,1)} %get-tuple-element.19), channel_id=1, source_target_pairs={{0,3},{1,0},{2,1},{3,2},{4,7},{5,4},{6,5},{7,6},{8,11},{9,8},{10,9... | collective-permute-start | bytes 3342344 | tf_op jit(solution)/shard_map/ppermute | solution.py:113
  43.8 26.3 %collective-permute-start.3 = (bf16[2,272,1024]{2,1,0:T(8,128)(2,1)}, bf16[2,272,1024]{2,1,0:T(8,128)(2,1)}, u32[]{:S(2)}, u32[]{:S(2)}) collective-permute-start(bf16[2,272,1024]{2,1,0:T(8,128)(2,1)} %get-tuple-element.21), channel_id=1, source_target_pairs={{0,2},{1,3},{2,0},{3,1},{4,6},{5,7},{6,4},{7,5},{8,10},{9,11},{10,... | collective-permute-start | bytes 3342344 | tf_op jit(solution)/shard_map/ppermute | solution.py:113
  45.5 94.6 %collective-permute-start.5 = (bf16[256,8,256]{0,2,1:T(8,128)(2,1)}, bf16[256,8,256]{0,2,1:T(8,128)(2,1)}, u32[]{:S(2)}, u32[]{:S(2)}) collective-permute-start(bf16[256,8,256]{0,2,1:T(8,128)(2,1)} %select_bitcast_fusion.2), channel_id=1, source_target_pairs={{0,16},{16,0},{1,17},{17,1},{2,18},{18,2},{3,19},{19,3},{4,20},{20... | collective-permute-start | bytes 3145736 | tf_op jit(solution)/shard_map/ppermute | solution.py:182
  51.5 44.7 %collective-permute-start.2 = (bf16[2,272,1024]{2,1,0:T(8,128)(2,1)}, bf16[2,272,1024]{2,1,0:T(8,128)(2,1)}, u32[]{:S(2)}, u32[]{:S(2)}) collective-permute-start(bf16[2,272,1024]{2,1,0:T(8,128)(2,1)} %get-tuple-element.20), channel_id=1, source_target_pairs={{0,1},{1,2},{2,3},{3,0},{4,5},{5,6},{6,7},{7,4},{8,9},{9,10},{10,1... | collective-permute-start | bytes 3342344 | tf_op jit(solution)/shard_map/ppermute | solution.py:113
  65.3 32.2 %copy-start.2 = (bf16[272,1024]{1,0:T(8,128)(2,1)}, bf16[272,1024]{1,0:T(8,128)(2,1)S(1)}, u32[]{:S(2)}) copy-start(bf16[272,1024]{1,0:T(8,128)(2,1)S(1)} %get-tuple-element.22.refs_7_) | copy-start | bytes 1671172
  65.3 32.2 %copy-start.3 = (bf16[272,1024]{1,0:T(8,128)(2,1)}, bf16[272,1024]{1,0:T(8,128)(2,1)S(1)}, u32[]{:S(2)}) copy-start(bf16[272,1024]{1,0:T(8,128)(2,1)S(1)} %get-tuple-element.23.refs_3_) | copy-start | bytes 1671172
  71.4 26.1 %copy-start.4 = (bf16[272,1024]{1,0:T(8,128)(2,1)}, bf16[272,1024]{1,0:T(8,128)(2,1)S(1)}, u32[]{:S(2)}) copy-start(bf16[272,1024]{1,0:T(8,128)(2,1)S(1)} %get-tuple-element.24.refs_6_) | copy-start | bytes 1671172
  71.4 26.1 %copy-start.5 = (bf16[272,1024]{1,0:T(8,128)(2,1)}, bf16[272,1024]{1,0:T(8,128)(2,1)S(1)}, u32[]{:S(2)}) copy-start(bf16[272,1024]{1,0:T(8,128)(2,1)S(1)} %get-tuple-element.25.refs_2_) | copy-start | bytes 1671172
  97.5 0.8 copy-start.6
  97.5 1.1 copy-start.7
  116.9 25.7 %collective-permute-start.6 = (bf16[256,2048]{1,0:T(8,128)(2,1)}, bf16[256,2048]{1,0:T(8,128)(2,1)S(1)}, u32[]{:S(2)}, u32[]{:S(2)}) collective-permute-start(bf16[256,2048]{1,0:T(8,128)(2,1)} %shard_map.55), channel_id=1, source_target_pairs={{0,16},{16,0},{1,17},{17,1},{2,18},{18,2},{3,19},{19,3},{4,20},{20... | collective-permute-start | bytes 3145736 | tf_op jit(solution)/shard_map/ppermute | solution.py:184
  142.6 9.9 %copy-start.9 = (bf16[256,2048]{1,0:T(8,128)(2,1)S(1)}, bf16[256,2048]{1,0:T(8,128)(2,1)}, u32[]{:S(2)}) copy-start(bf16[256,2048]{1,0:T(8,128)(2,1)} %shard_map.55) | copy-start | bytes 3145732
  142.6 9.9 %copy-start.11 = (bf16[16384,256]{1,0:T(8,128)(2,1)S(1)}, bf16[16384,256]{1,0:T(8,128)(2,1)}, u32[]{:S(2)}) copy-start(bf16[16384,256]{1,0:T(8,128)(2,1)} %all-gather.3.cloned.1.call-done) | copy-start | bytes 25165828
  149.7 2.7 %collective-permute-start.7 = (bf16[256,8,256]{0,2,1:T(8,128)(2,1)S(1)}, bf16[256,8,256]{0,2,1:T(8,128)(2,1)S(1)}, u32[]{:S(2)}, u32[]{:S(2)}) collective-permute-start(bf16[256,8,256]{0,2,1:T(8,128)(2,1)S(1)} %add_convert_fusion), channel_id=1, source_target_pairs={{0,16},{16,0},{1,17},{17,1},{2,18},{18,2},{3,19},{19,3},{4,20},{20... | collective-permute-start | bytes 3145736 | tf_op jit(solution)/shard_map/ppermute | solution.py:194
Sparse Core Ops, SparseCore 0:
  9.1 92.2 all-gather.2
where the time goes:
time: 167 us; the launch traced here: 166 us
  waiting for transfers between devices  63.2 us (38%)
  starting transfers between devices  33.6 us (20%)
  between operations  24.5 us (15%)
  local copies, waits for them, and re-layouts  22.9 us (14%)
  matrix products  10.9 us (7%)
  Pallas kernels  7.18 us (4%)
  other arithmetic  4.1 us (2%)
    ppermute x3, waiting for transfers between devices, tokens_attention(): got = lax.ppermute(sent, 'help', pairs)  34.5 us
    ppermute x1, starting transfers between devices, on_device(): partner_att = lax.ppermute(attended, 'core', partner)  23.2 us
    ppermute x1, waiting for transfers between devices, tokens_attention(): lax.ppermute(packed, 'help', [(j, j + 2 * across) for j in range(help_siz...  11.8 us
    ppermute x1, waiting for transfers between devices, tokens_attention(): lax.ppermute(packed, 'help', [(j, j + across) for j in range(help_size -...  11.4 us
    dot_general x2, matrix products, project(): jnp.einsum('qk,zkn->qzn', rows, gathered, preferred_element_type=jnp.floa...  10.9 us
    unnamed x27, local copies, waits for them, and re-layouts  7.98 us
    pallas_call x1, Pallas kernels, tokens_attention(): pl.pallas_call(kernel, grid_spec=grid_spec, out_shape=jax.ShapeDtypeStruc...  7.18 us
    slice x8, local copies, waits for them, and re-layouts, tokens_attention(): segk[s, local_rows - 1] >= first_seg  5.3 us
  transfers between devices with their start and end apart: 9, of which 7 were waited for; matrix products, arithmetic and copies ran while one was open for 14% of the time, Pallas kernels for 4%

commit v1 on v0

--- a/solution.py
+++ b/solution.py
@@ -99,7 +99,7 @@
         packed, "help", [(j, j + 2 * across) for j in range(help_size - 2 * across)]
     )
     column = helper % across
-    pieces = {0: packed, across: one_back, 2 * across: two_back}
+    pieces = {0: (packed, None), across: (one_back, None), 2 * across: (two_back, None)}
     for k in range(1, across):
         pairs = [
             (y * across + x, y * across + (x + k) % across)
@@ -111,13 +111,17 @@
             wraps, jnp.stack([one_back, two_back]), jnp.stack([packed, one_back])
         )
         got = lax.ppermute(sent, "help", pairs)
-        pieces[k] = got[0]
-        pieces[k + across] = got[1]
+        pieces[k] = (got, 0)
+        pieces[k + across] = (got, 1)
     received = [pieces[s] for s in range(reach + 1)]
     blocks = len(received)
-    segk = jnp.stack(
-        [seg_local] + [r[local_rows, :local_rows].astype(jnp.int32) for r in received[1:]]
-    )
+
+    def seg_of(piece):
+        array, index = piece
+        row = array[local_rows] if index is None else array[index, local_rows]
+        return row[:local_rows].astype(jnp.int32)
+
+    segk = jnp.stack([seg_local] + [seg_of(p) for p in received[1:]])
     first_seg = seg_local[0]
     flags = jnp.stack(
         [jnp.int32(1)]
@@ -142,7 +146,12 @@
             pl.BlockSpec((local_rows, 1), lambda g, f: (0, 0)),
             pl.BlockSpec((blocks, local_rows), lambda g, f: (0, 0)),
         ]
-        + [pl.BlockSpec((local_rows, pair), lambda g, f: (0, g)) for _ in range(blocks)],
+        + [
+            pl.BlockSpec((local_rows, pair), lambda g, f: (0, g))
+            if index is None
+            else pl.BlockSpec((None, local_rows, pair), lambda g, f, i=index: (i, 0, g))
+            for _, index in received
+        ],
         out_specs=pl.BlockSpec((local_rows, width), lambda g, f: (0, g)),
         scratch_shapes=[
             pltpu.VMEM((group_size * local_rows, 128), jnp.float32),
@@ -160,7 +169,7 @@
         queries.reshape(local_rows, heads * head_dim),
         seg_local.reshape(local_rows, 1),
         segk,
-        *received,
+        *[array for array, _ in received],
     )
 
 
@@ -192,9 +201,12 @@
         mine = project(attended, own_cols)
         theirs = project(partner_att, partner_res)
         back = lax.ppermute(theirs, "core", partner)
-        col0 = jnp.where(first, mine, back)
-        col1 = jnp.where(first, back, mine)
-        return jnp.stack([col0, col1], axis=2).reshape(local_rows, planes * 2 * width)
+        joined = lax.cond(
+            first,
+            lambda: jnp.stack([mine, back], axis=2),
+            lambda: jnp.stack([back, mine], axis=2),
+        )
+        return joined.reshape(local_rows, planes * 2 * width)
 
     return on_device
 

time: 167 us -> 168 us (level)
  the two profiles are of different devices: /device:TPU:241 before, /device:TPU:83 now
where the time goes in v1:
time: 168 us; the launch traced here: 167 us
  waiting for transfers between devices  57.1 us (34%)
  Pallas kernels  29.7 us (18%)
  local copies, waits for them, and re-layouts  26.3 us (16%)
  between operations  23.6 us (14%)
  matrix products  13 us (8%)
  starting transfers between devices  9.96 us (6%)
  other arithmetic  7.3 us (4%)
    ppermute x3, waiting for transfers between devices, tokens_attention(): got = lax.ppermute(sent, 'help', pairs)  30.5 us
    pallas_call x1, Pallas kernels, tokens_attention(): pl.pallas_call(kernel, grid_spec=grid_spec, out_shape=jax.ShapeDtypeStruc...  29.7 us
    dot_general x2, matrix products, project(): jnp.einsum('qk,zkn->qzn', rows, gathered, preferred_element_type=jnp.floa...  13 us
    ppermute x1, waiting for transfers between devices, tokens_attention(): lax.ppermute(packed, 'help', [(j, j + 2 * across) for j in range(help_siz...  11.7 us
    ppermute x1, waiting for transfers between devices, tokens_attention(): lax.ppermute(packed, 'help', [(j, j + across) for j in range(help_size -...  11.4 us
    unnamed x21, local copies, waits for them, and re-layouts  9.82 us
    slice x8, local copies, waits for them, and re-layouts, tokens_attention(): segk[s, local_rows - 1] >= first_seg  5.07 us
    another operation x2, local copies, waits for them, and re-layouts, on_device(): jnp.stack([back, mine], axis=2)  4.42 us
  transfers between devices with their start and end apart: 9, of which 6 were waited for; matrix products, arithmetic and copies ran while one was open for 19% of the time, Pallas kernels for 18%

profile of v1, /device:TPU:83, one launch (start us, length us, event | category | flops | bytes accessed | tf_op | source)
XLA Modules:
  0.0 167.0 jit_solution(12334548523467190531)
XLA Ops:
  6.5 0.7 all-gather.3.cloned.1.call-update
  7.3 1.1 copy.26
  8.4 0.1 fusion.14
  8.6 2.9 %collective-permute-start.1 = (bf16[272,1024]{1,0:T(8,128)(2,1)S(1)}, bf16[272,1024]{1,0:T(8,128)(2,1)S(1)}, u32[]{:S(2)}, u32[]{:S(2)}) collective-permute-start(bf16[272,1024]{1,0:T(8,128)(2,1)S(1)} %get-tuple-element.58.refs_0_), channel_id=1, source_target_pairs={{0,4},{1,5},{2,6},{3,7},{4,8},{5,9},{6,10},{7,11},{8,12},{9,13},{1... | collective-permute-start | bytes 1671176 | tf_op jit(solution)/shard_map/ppermute | solution.py:95
  11.5 1.3 collective-permute-start.2
  12.8 11.4 %collective-permute-done.1.refs_4_ = bf16[272,1024]{1,0:T(8,128)(2,1)S(1)} collective-permute-done((bf16[272,1024]{1,0:T(8,128)(2,1)S(1)}, bf16[272,1024]{1,0:T(8,128)(2,1)S(1)}, u32[]{:S(2)}, u32[]{:S(2)}) %collective-permute-start.1) | collective-permute-done | bytes 557088 | tf_op jit(solution)/shard_map/ppermute | solution.py:95
  24.2 11.7 %collective-permute-done.2.refs_8_ = bf16[272,1024]{1,0:T(8,128)(2,1)S(1)} collective-permute-done((bf16[272,1024]{1,0:T(8,128)(2,1)S(1)}, bf16[272,1024]{1,0:T(8,128)(2,1)S(1)}, u32[]{:S(2)}, u32[]{:S(2)}) %collective-permute-start.2) | collective-permute-done | bytes 557088 | tf_op jit(solution)/shard_map/ppermute | solution.py:98
  35.8 2.0 %broadcast_select_fusion = (bf16[2,272,1024]{2,1,0:T(8,128)(2,1)}, bf16[2,272,1024]{2,1,0:T(8,128)(2,1)}, bf16[2,272,1024]{2,1,0:T(8,128)(2,1)}) fusion(pred[]{:T(512)S(6)} %ge.90, bf16[1,272,1024]{2,1,0:T(8,128)(2,1)S(1)} %bitcast.84, bf16[1,272,1024]{2,1,0:T(8,128)(2,1)S(1)} %get-tuple-element.57, bf16[1,272,1024]{2,1,0:T(8,128)(2,1)S(1)} %bitcast.85, ...), kind=kLoop, calls=%fused_computation.13 | loop fusion | flops 2785280 | bytes 5013507 | tf_op jit(solution)/shard_map/jit(_where)/select_n | solution.py:110
  37.9 1.3 collective-permute-start.3
  39.2 3.3 %copy.16 = bf16[256,4096]{0,1:T(8,128)(2,1)S(1)} copy(bf16[256,4096]{1,0:T(8,128)(2,1)} %param.12) | data formatting | bytes 4194304 | tf_op args[3]
  42.5 0.9 collective-permute-start.4
  43.4 1.5 fusion.15
  44.9 1.6 copy.24
  46.4 1.3 copy.25
  47.8 1.9 %collective-permute-start.5 = (bf16[2,272,1024]{2,1,0:T(8,128)(2,1)}, bf16[2,272,1024]{2,1,0:T(8,128)(2,1)S(1)}, u32[]{:S(2)}, u32[]{:S(2)}) collective-permute-start(bf16[2,272,1024]{2,1,0:T(8,128)(2,1)} %get-tuple-element.48), channel_id=1, source_target_pairs={{0,3},{1,0},{2,1},{3,2},{4,7},{5,4},{6,5},{7,6},{8,11},{9,8},{10,9... | collective-permute-start | bytes 3342344 | tf_op jit(solution)/shard_map/ppermute | solution.py:113
  49.7 2.3 %select_bitcast_fusion = bf16[256,8,256]{2,0,1:T(8,128)(2,1)} fusion(bf16[256,8,1,256]{3,0,1,2:T(8,128)(2,1)S(1)} %copy.24, bf16[256,8,1,256]{3,0,1,2:T(8,128)(2,1)} %copy.25, pred[]{:T(512)S(6)} %eq.5), kind=kLoop, calls=%fused_computation.20 | loop fusion | flops 524288 | bytes 3145729 | tf_op jit(solution)/shard_map/jit(_where)/select_n | solution.py:190
  52.0 1.3 collective-permute-start
  53.2 0.6 slice.104
  53.8 2.5 %copy.33 = bf16[32,8,16,128]{3,1,2,0:T(8,128)(2,1)} copy(bf16[32,8,16,128]{3,2,1,0:T(8,128)(2,1)} %bitcast.87) | data formatting | bytes 2097152
  56.3 0.8 copy.19.segq_ref
  57.1 0.7 slice_convert_fusion.1
  57.8 0.6 slice.128
  58.4 0.7 slice_convert_fusion
  59.1 0.7 slice.136
  62.2 0.5 collective-permute-done.3.refs_1_.refs_5_
  62.7 0.7 slice.122
  63.4 5.1 %collective-permute-done.4.refs_2_.refs_6_ = bf16[2,272,1024]{2,1,0:T(8,128)(2,1)} collective-permute-done((bf16[2,272,1024]{2,1,0:T(8,128)(2,1)}, bf16[2,272,1024]{2,1,0:T(8,128)(2,1)}, u32[]{:S(2)}, u32[]{:S(2)}) %collective-permute-start.4) | collective-permute-done | bytes 1114144 | tf_op jit(solution)/shard_map/ppermute | solution.py:113
  68.6 0.7 fusion.9
  69.3 0.6 slice.124
  69.9 24.9 %collective-permute-done.5.refs_3_.refs_7_ = bf16[2,272,1024]{2,1,0:T(8,128)(2,1)S(1)} collective-permute-done((bf16[2,272,1024]{2,1,0:T(8,128)(2,1)}, bf16[2,272,1024]{2,1,0:T(8,128)(2,1)S(1)}, u32[]{:S(2)}, u32[]{:S(2)}) %collective-permute-start.5) | collective-permute-done | bytes 1114144 | tf_op jit(solution)/shard_map/ppermute | solution.py:113
  94.7 0.7 slice.126
  95.4 0.6 slice.130
  96.0 0.6 slice.132
  96.7 1.2 stack.109.segk_ref
  97.9 0.6 slice.134
  106.0 0.1 stack.107
  106.1 0.6 stack.108.flags_ref
  106.7 29.7 %shard_map.57 = bf16[256,2048]{1,0:T(8,128)(2,1)} custom-call(s32[9]{0:T(128)} %stack.108.flags_ref, bf16[256,2048]{1,0:T(8,128)(2,1)} %bitcast.83, s32[256,1]{1,0:T(8,128)} %copy.19.segq_ref, s32[9,256]{1,0:T(8,128)} %stack.109.segk_ref, bf16[272,1024]{1,0:T(8,128)(2,1)} %copy-done.6, bf16[2,272,1024]{2,1,0:T(8,128)(2,1)} %copy-done, ...), custom_call_target="tpu_custom_call" | custom-call | tf_op jit(solution)/shard_map/pallas_call | solution.py:161
  136.4 0.3 collective-permute-start.6
  136.7 2.8 %collective-permute-done.6 = bf16[256,2048]{1,0:T(8,128)(2,1)S(1)} collective-permute-done((bf16[256,2048]{1,0:T(8,128)(2,1)}, bf16[256,2048]{1,0:T(8,128)(2,1)S(1)}, u32[]{:S(2)}, u32[]{:S(2)}) %collective-permute-start.6) | collective-permute-done | bytes 1048608 | tf_op jit(solution)/shard_map/ppermute | solution.py:193
  139.5 7.0 %add_convert_fusion = bf16[256,8,256]{2,0,1:T(8,128)(2,1)} fusion(bf16[256,8,256]{2,0,1:T(8,128)(2,1)} %collective-permute-done, bf16[8,2048,256]{2,1,0:T(8,128)(2,1)} %bitcast.90, bf16[256,2048]{1,0:T(8,128)(2,1)S(1)} %collective-permute-done.6), kind=kOutput, calls=%fused_computation.8 | convolution fusion | flops 2149056512 | bytes 11534336 | tf_op jit(solution)/shard_map/qk,zkn->qzn/dot_general | solution.py:196
  146.5 0.1 collective-permute-start.7
  146.7 6.0 %fusion = bf16[256,8,256]{2,0,1:T(8,128)(2,1)S(1)} fusion(bf16[8,2048,256]{2,1,0:T(8,128)(2,1)} %bitcast.91, bf16[256,2048]{1,0:T(8,128)(2,1)} %shard_map.57, bf16[256,8,1,256]{3,0,1,2:T(8,128)(2,1)S(1)} %copy-done.2, bf16[256,8,1,256]{3,0,1,2:T(8,128)(2,1)S(1)} %copy.24, pred[]{:T(512)S(6)} %eq.5), kind=kOutput, calls=%fused_computation.7 | convolution fusion | flops 2149580800 | bytes 12582913 | tf_op jit(solution)/shard_map/qk,zkn->qzn/dot_general | solution.py:196
  152.7 7.4 %conditional.1 = (bf16[256,4096]{1,0:T(8,128)(2,1)}) conditional(s32[]{:T(128)} %convert_element_type.116, (bf16[256,8,256]{2,0,1:T(8,128)(2,1)S(1)}, bf16[256,8,256]{2,0,1:T(8,128)(2,1)S(1)}) %tuple.17, (bf16[256,8,256]{2,0,1:T(8,128)(2,1)S(1)}, bf16[256,8,256]{2,0,1:T(8,128)(2,1)S(1)}) %tuple.18), branch_computations={%region_0.1_spmd, %region_1.2_spmd} | conditional | flops 1048576 | bytes 16777224 | solution.py:204
  152.8 1.2 copy_bitcast_fusion
  153.9 0.2 pad_maximum_fusion
  154.1 3.2 %copy.14 = bf16[256,8,2,256]{3,2,1,0:T(2,128)(2,1)S(1)} copy(bf16[256,8,2,256]{3,1,0,2:T(8,128)(2,1)S(1)} %pad_maximum_fusion) | data formatting | bytes 4194304 | tf_op jit(solution)/shard_map/cond/branch_0_fun/stack | solution.py:207
  157.4 2.8 %reshape.136 = bf16[256,4096]{1,0:T(8,128)(2,1)} reshape(bf16[256,8,2,256]{3,2,1,0:T(2,128)(2,1)S(1)} %copy.14) | data formatting | bytes 4194304 | tf_op jit(solution)/shard_map/reshape | solution.py:209
  (23 shorter events, 0.1 us)
Async XLA Ops:
  6.5 1.9 %copy-start.7 = (s32[1,256]{1,0:T(1,128)S(1)}, s32[1,256]{1,0:T(1,128)}, u32[]{:S(2)}) copy-start(s32[1,256]{1,0:T(1,128)} %param.11) | copy-start | bytes 3076
  6.5 133.0 %all-gather.3.cloned.1.call-start = ((), (), s32[]{:S(2)}) async-start(), calls=%async_computation | async-start | bytes 9437184 | tf_op jit(solution)/shard_map/all_gather | solution.py:182
  8.6 29.3 %copy-start.6 = (bf16[272,1024]{1,0:T(8,128)(2,1)}, bf16[272,1024]{1,0:T(8,128)(2,1)S(1)}, u32[]{:S(2)}) copy-start(bf16[272,1024]{1,0:T(8,128)(2,1)S(1)} %get-tuple-element.58.refs_0_) | copy-start | bytes 1671172
  8.6 15.6 %collective-permute-start.1 = (bf16[272,1024]{1,0:T(8,128)(2,1)S(1)}, bf16[272,1024]{1,0:T(8,128)(2,1)S(1)}, u32[]{:S(2)}, u32[]{:S(2)}) collective-permute-start(bf16[272,1024]{1,0:T(8,128)(2,1)S(1)} %get-tuple-element.58.refs_0_), channel_id=1, source_target_pairs={{0,4},{1,5},{2,6},{3,7},{4,8},{5,9},{6,10},{7,11},{8,12},{9,13},{1... | collective-permute-start | bytes 1671176 | tf_op jit(solution)/shard_map/ppermute | solution.py:95
  11.5 24.4 %collective-permute-start.2 = (bf16[272,1024]{1,0:T(8,128)(2,1)S(1)}, bf16[272,1024]{1,0:T(8,128)(2,1)S(1)}, u32[]{:S(2)}, u32[]{:S(2)}) collective-permute-start(bf16[272,1024]{1,0:T(8,128)(2,1)S(1)} %get-tuple-element.58.refs_0_), channel_id=1, source_target_pairs={{0,8},{1,9},{2,10},{3,11},{4,12},{5,13},{6,14},{7,15},{16,24},{17,... | collective-permute-start | bytes 1671176 | tf_op jit(solution)/shard_map/ppermute | solution.py:98
  24.2 13.7 %copy-start.4 = (bf16[272,1024]{1,0:T(8,128)(2,1)}, bf16[272,1024]{1,0:T(8,128)(2,1)S(1)}, u32[]{:S(2)}) copy-start(bf16[272,1024]{1,0:T(8,128)(2,1)S(1)} %collective-permute-done.1.refs_4_) | copy-start | bytes 1671172
  35.8 2.0 %copy-start.5 = (bf16[272,1024]{1,0:T(8,128)(2,1)}, bf16[272,1024]{1,0:T(8,128)(2,1)S(1)}, u32[]{:S(2)}) copy-start(bf16[272,1024]{1,0:T(8,128)(2,1)S(1)} %collective-permute-done.2.refs_8_) | copy-start | bytes 1671172
  37.9 24.8 %collective-permute-start.3 = (bf16[2,272,1024]{2,1,0:T(8,128)(2,1)}, bf16[2,272,1024]{2,1,0:T(8,128)(2,1)S(1)}, u32[]{:S(2)}, u32[]{:S(2)}) collective-permute-start(bf16[2,272,1024]{2,1,0:T(8,128)(2,1)} %get-tuple-element.49), channel_id=1, source_target_pairs={{0,1},{1,2},{2,3},{3,0},{4,5},{5,6},{6,7},{7,4},{8,9},{9,10},{10,1... | collective-permute-start | bytes 3342344 | tf_op jit(solution)/shard_map/ppermute | solution.py:113
  42.5 26.1 %collective-permute-start.4 = (bf16[2,272,1024]{2,1,0:T(8,128)(2,1)}, bf16[2,272,1024]{2,1,0:T(8,128)(2,1)}, u32[]{:S(2)}, u32[]{:S(2)}) collective-permute-start(bf16[2,272,1024]{2,1,0:T(8,128)(2,1)} %get-tuple-element.50), channel_id=1, source_target_pairs={{0,2},{1,3},{2,0},{3,1},{4,6},{5,7},{6,4},{7,5},{8,10},{9,11},{10,... | collective-permute-start | bytes 3342344 | tf_op jit(solution)/shard_map/ppermute | solution.py:113
  44.9 1.6 copy-start.3
  47.8 46.9 %collective-permute-start.5 = (bf16[2,272,1024]{2,1,0:T(8,128)(2,1)}, bf16[2,272,1024]{2,1,0:T(8,128)(2,1)S(1)}, u32[]{:S(2)}, u32[]{:S(2)}) collective-permute-start(bf16[2,272,1024]{2,1,0:T(8,128)(2,1)} %get-tuple-element.48), channel_id=1, source_target_pairs={{0,3},{1,0},{2,1},{3,2},{4,7},{5,4},{6,5},{7,6},{8,11},{9,8},{10,9... | collective-permute-start | bytes 3342344 | tf_op jit(solution)/shard_map/ppermute | solution.py:113
  52.0 84.7 %collective-permute-start = (bf16[256,8,256]{2,0,1:T(8,128)(2,1)}, bf16[256,8,256]{2,0,1:T(8,128)(2,1)}, u32[]{:S(2)}, u32[]{:S(2)}) collective-permute-start(bf16[256,8,256]{2,0,1:T(8,128)(2,1)} %select_bitcast_fusion), channel_id=1, source_target_pairs={{0,16},{16,0},{1,17},{17,1},{2,18},{18,2},{3,19},{19,3},{4,20},{20... | collective-permute-start | bytes 3145736 | tf_op jit(solution)/shard_map/ppermute | solution.py:191
  62.7 44.0 %copy-start = (bf16[2,272,1024]{2,1,0:T(8,128)(2,1)}, bf16[2,272,1024]{2,1,0:T(8,128)(2,1)S(1)}, u32[]{:S(2)}) copy-start(bf16[2,272,1024]{2,1,0:T(8,128)(2,1)S(1)} %collective-permute-done.3.refs_1_.refs_5_) | copy-start | bytes 3342340
  94.7 12.0 %copy-start.1 = (bf16[2,272,1024]{2,1,0:T(8,128)(2,1)}, bf16[2,272,1024]{2,1,0:T(8,128)(2,1)S(1)}, u32[]{:S(2)}) copy-start(bf16[2,272,1024]{2,1,0:T(8,128)(2,1)S(1)} %collective-permute-done.5.refs_3_.refs_7_) | copy-start | bytes 3342340
  136.4 3.1 %collective-permute-start.6 = (bf16[256,2048]{1,0:T(8,128)(2,1)}, bf16[256,2048]{1,0:T(8,128)(2,1)S(1)}, u32[]{:S(2)}, u32[]{:S(2)}) collective-permute-start(bf16[256,2048]{1,0:T(8,128)(2,1)} %shard_map.57), channel_id=1, source_target_pairs={{0,16},{16,0},{1,17},{17,1},{2,18},{18,2},{3,19},{19,3},{4,20},{20... | collective-permute-start | bytes 3145736 | tf_op jit(solution)/shard_map/ppermute | solution.py:193
  139.5 7.1 %copy-start.2 = (bf16[256,8,1,256]{3,0,1,2:T(8,128)(2,1)S(1)}, bf16[256,8,1,256]{3,0,1,2:T(8,128)(2,1)}, u32[]{:S(2)}) copy-start(bf16[256,8,1,256]{3,0,1,2:T(8,128)(2,1)} %copy.25) | copy-start | bytes 3145732
  146.5 6.2 %collective-permute-start.7 = (bf16[256,8,256]{2,0,1:T(8,128)(2,1)}, bf16[256,8,256]{2,0,1:T(8,128)(2,1)S(1)}, u32[]{:S(2)}, u32[]{:S(2)}) collective-permute-start(bf16[256,8,256]{2,0,1:T(8,128)(2,1)} %add_convert_fusion), channel_id=1, source_target_pairs={{0,16},{16,0},{1,17},{17,1},{2,18},{18,2},{3,19},{19,3},{4,20},{20... | collective-permute-start | bytes 3145736 | tf_op jit(solution)/shard_map/ppermute | solution.py:203
Sparse Core Ops, SparseCore 0:
  9.1 94.1 all-gather.2
